TPU v7x, 128 devices: a whole 4x4x4 slice. The times are simulated.
128 devices in a mesh: req: 8 (over y, core), exp: 16 (over z, x).
Axes of the slice: x: 4, y: 4, z: 4, core: 2. Of those that a mesh axis runs over, the one named last changes fastest.
Arguments:
- hidden: bfloat16 [16384, 2560], P(('req', 'exp')), may hold values from -1.5 to 1.5
- queries: bfloat16 [16384, 1280], P(('req', 'exp')), may hold values from -100 to 100
- suffix_kv: bfloat16 [16384, 512], P(('req', 'exp')), may hold values from -24 to 24
- lengths: int32 [8, 4], P('req'), may hold values from 1 to 1024, 2048 in all within a row
- page_table: int32 [8, 4, 32], P('req'), may hold values from 0 to 55
- page_pool: bfloat16 [56, 128, 512], P('req'), may hold values from -24 to 24
- w_out: bfloat16 [1280, 2560], replicated, may hold values from -0.15625 to 0.15625
- w_router: bfloat16 [2560, 64], replicated, may hold values from -5 to 5
- routes: int32 [16384, 6], P(('req', 'exp')), may hold values from 0 to 63, all different within a row; in each aligned block of 128 rows (0 to 127, 128 to 255, ...) at most 15 rows name the same one
- w_gate: bfloat16 [128, 2560, 768], P(('req', 'exp')), may hold values from -0.125 to 0.125
- w_up: bfloat16 [128, 2560, 768], P(('req', 'exp')), may hold values from -0.125 to 0.125
- w_down: bfloat16 [128, 768, 2560], P(('req', 'exp')), may hold values from -0.4375 to 0.4375
Outputs:
- layer_out: bfloat16 [16384, 2560], P(('req', 'exp'))
Inputs may be any that keep to these rules, and one draw needn't show every extreme that they name: `lengths`: each row sums to 2048; its largest entry is exactly 1024. `page_table`: a page may appear in several prefixes and more than once in one. `routes`: the 6 experts of a token are distinct; among the rows of one device no expert is named more than 15 times, a bound that some block reaches.
All inputs are finite; a program needn't handle non-finite values.
Results may differ from a plain program's by a relative error of at most 0.022.
Values may be sent and summed in bfloat16 or wider, within the bound.
No kernel may reach another device: no remote copies, remote signals or barrier semaphores. Data moves between devices by JAX's collectives and lax.ppermute only.
A program may use at most 192 MiB of HBM per device.

v0:
```python
import math
import jax
import jax.numpy as jnp
from jax import lax
from jax.sharding import PartitionSpec as P

D = 2560
QUERY_HEADS = 10
KEY_VALUE_HEADS = 2
HEAD_SIZE = 128
TOP = 6
PAGE_TOKENS = 128
NEGATIVE_MASK = -1e30
EPS = 1e-06


def fold_scores(carry, query_matrix, key_rows, value_rows, weights):
    scores = jnp.einsum(
        "tgrd,kgd->tgrk", query_matrix, key_rows, preferred_element_type=jnp.float32
    ) * (1.0 / math.sqrt(HEAD_SIZE))
    running_maximum, grand_total, summed_output = carry
    live = weights[:, None, None, :] > 0
    fresh = jnp.maximum(running_maximum, jnp.max(jnp.where(live, scores, NEGATIVE_MASK), axis=-1))
    expo = jnp.where(live, jnp.exp(scores - fresh[..., None]), 0.0) * weights[:, None, None, :]
    decay = jnp.exp(running_maximum - fresh)
    grand_total = decay * grand_total + jnp.sum(expo, axis=-1)
    summed_output = decay[..., None] * summed_output + jnp.einsum(
        "tgrk,kgd->tgrd", expo.astype(jnp.bfloat16), value_rows, preferred_element_type=jnp.float32
    )
    return (fresh, grand_total, summed_output)


def empty_carry(token_count, request_groups):
    return (
        jnp.full((token_count, KEY_VALUE_HEADS, request_groups), NEGATIVE_MASK, jnp.float32),
        jnp.zeros((token_count, KEY_VALUE_HEADS, request_groups), jnp.float32),
        jnp.zeros((token_count, KEY_VALUE_HEADS, request_groups, HEAD_SIZE), jnp.float32),
    )


def on_device(
    hidden,
    queries,
    suffix_kv,
    lengths,
    page_table,
    page_pool,
    w_out,
    w_router,
    routes,
    w_gate,
    w_up,
    w_down,
):
    token_index = hidden.shape[0]
    row_width = KEY_VALUE_HEADS * HEAD_SIZE
    request_groups = QUERY_HEADS // KEY_VALUE_HEADS
    request_count = lax.axis_size("req")
    pool_per_shard = page_pool.shape[0]
    pool_all = pool_per_shard * request_count
    query_matrix = queries.reshape(token_index, KEY_VALUE_HEADS, request_groups, HEAD_SIZE)
    positions = lax.axis_index("exp") * token_index + jnp.arange(token_index, dtype=jnp.int32)
    lens = lengths[0]
    ends = jnp.cumsum(lens)
    starts = ends - lens
    req_of = jnp.sum((positions[:, None] >= ends[None, :]).astype(jnp.int32), axis=1)
    pick = req_of[:, None] == jnp.arange(lens.shape[0], dtype=jnp.int32)[None, :]
    first = jnp.sum(jnp.where(pick, starts[None, :], 0), axis=1)
    counts = jnp.sum(
        (page_table[0][:, :, None] == jnp.arange(pool_all, dtype=jnp.int32)[None, None, :]).astype(
            jnp.float32
        ),
        axis=1,
    )
    query_counts = jnp.dot(pick.astype(jnp.float32), counts, precision=lax.Precision.HIGHEST)
    query_total_set, every_count = (
        lax.all_gather(queries, "req", axis=0, tiled=True),
        lax.all_gather(query_counts.astype(jnp.bfloat16), "req", axis=0, tiled=True),
    )
    query_total_count = query_total_set.shape[0]
    local = lax.dynamic_slice_in_dim(
        every_count, lax.axis_index("req") * pool_per_shard, pool_per_shard, 1
    ).astype(jnp.float32)
    weights = jnp.repeat(local, PAGE_TOKENS, axis=1)
    flattened = page_pool.reshape(pool_per_shard * PAGE_TOKENS, 2 * row_width)
    key_rows = flattened[:, :row_width].reshape(
        pool_per_shard * PAGE_TOKENS, KEY_VALUE_HEADS, HEAD_SIZE
    )
    value_rows = flattened[:, row_width:].reshape(
        pool_per_shard * PAGE_TOKENS, KEY_VALUE_HEADS, HEAD_SIZE
    )
    running_maximum, grand_total, summed_output = fold_scores(
        empty_carry(query_total_count, request_groups),
        query_total_set.reshape(query_total_count, KEY_VALUE_HEADS, request_groups, HEAD_SIZE),
        key_rows,
        value_rows,
        weights,
    )
    peaks, totals, sums = (
        lax.all_to_all(
            running_maximum.reshape(request_count, token_index, KEY_VALUE_HEADS, request_groups),
            "req",
            split_axis=0,
            concat_axis=0,
            tiled=True,
        ),
        lax.all_to_all(
            grand_total.reshape(request_count, token_index, KEY_VALUE_HEADS, request_groups),
            "req",
            split_axis=0,
            concat_axis=0,
            tiled=True,
        ),
        lax.all_to_all(
            summed_output.reshape(
                request_count, token_index, KEY_VALUE_HEADS, request_groups, HEAD_SIZE
            ),
            "req",
            split_axis=0,
            concat_axis=0,
            tiled=True,
        ),
    )
    highest = jnp.max(peaks, axis=0)
    factor = jnp.exp(peaks - highest[None])
    carry = (highest, jnp.sum(factor * totals, axis=0), jnp.sum(factor[..., None] * sums, axis=0))
    segment = lax.all_gather(suffix_kv, "exp", axis=0, tiled=True)
    token_count = segment.shape[0]
    keypos = jnp.arange(token_count, dtype=jnp.int32)
    weights = (
        (keypos[None, :] <= positions[:, None]) & (keypos[None, :] >= first[:, None])
    ).astype(jnp.float32)
    key_rows = segment[:, :row_width].reshape(token_count, KEY_VALUE_HEADS, HEAD_SIZE)
    value_rows = segment[:, row_width:].reshape(token_count, KEY_VALUE_HEADS, HEAD_SIZE)
    running_maximum, grand_total, summed_output = fold_scores(
        carry, query_matrix, key_rows, value_rows, weights
    )
    attended = (
        (summed_output / grand_total[..., None])
        .reshape(token_index, QUERY_HEADS * HEAD_SIZE)
        .astype(jnp.bfloat16)
    )
    projected = jnp.dot(attended, w_out, preferred_element_type=jnp.float32)
    resid = lax.optimization_barrier((hidden.astype(jnp.float32) + projected).astype(jnp.bfloat16))
    resid_f = resid.astype(jnp.float32)
    normed = (resid_f * lax.rsqrt(jnp.mean(resid_f * resid_f, axis=1, keepdims=True) + EPS)).astype(
        jnp.bfloat16
    )
    n_experts = w_router.shape[1]
    logits = jnp.dot(normed, w_router, preferred_element_type=jnp.float32)
    expert_ids = jnp.arange(n_experts, dtype=jnp.int32)
    chosen = jnp.sum(
        jnp.where(routes[:, :, None] == expert_ids[None, None, :], logits[:, None, :], 0.0), axis=2
    )
    gates = jax.nn.softmax(chosen, axis=1)
    capacity = 16
    member = routes[:, :, None] == expert_ids[None, None, :]
    picks = jnp.any(member, axis=1).astype(jnp.float32)
    gate_of = jnp.sum(jnp.where(member, gates[:, :, None], 0.0), axis=1)
    earlier = (
        jnp.arange(token_index, dtype=jnp.int32)[:, None]
        > jnp.arange(token_index, dtype=jnp.int32)[None, :]
    ).astype(jnp.float32)
    rank = jnp.dot(earlier, picks, precision=lax.Precision.HIGHEST).astype(jnp.int32)
    place = jnp.arange(capacity, dtype=jnp.int32)
    select = (picks[None, :, :] > 0) & (rank[None, :, :] == place[:, None, None])
    select = jnp.transpose(select, (2, 0, 1))
    select2 = jnp.broadcast_to(select[:, None], (n_experts, 2, capacity, token_index)).reshape(
        2 * n_experts * capacity, token_index
    )
    outgoing = jnp.dot(
        select2.astype(jnp.bfloat16), normed, preferred_element_type=jnp.float32
    ).astype(jnp.bfloat16)
    outgoing = outgoing.reshape(2 * n_experts, capacity, D)
    rows = lax.all_to_all(outgoing, ("req", "exp"), split_axis=0, concat_axis=0, tiled=True)
    array_shape = rows.shape
    flat_rows = rows.reshape(-1, D)
    gate_part = jnp.dot(flat_rows, w_gate[0], preferred_element_type=jnp.float32)
    up_part = jnp.dot(flat_rows, w_up[0], preferred_element_type=jnp.float32)
    inner = (jax.nn.silu(gate_part) * up_part).astype(jnp.bfloat16)
    returned = lax.all_to_all(
        jnp.dot(inner, w_down[0], preferred_element_type=jnp.float32)
        .astype(jnp.bfloat16)
        .reshape(array_shape),
        ("req", "exp"),
        split_axis=0,
        concat_axis=0,
        tiled=True,
    ).reshape(2 * n_experts * capacity, D)
    weight = jnp.where(
        jnp.transpose(select, (2, 0, 1))[:, :, None, :], gate_of[:, :, None, None], 0.0
    )
    weight = jnp.broadcast_to(weight, (token_index, n_experts, 2, capacity)).reshape(
        token_index, 2 * n_experts * capacity
    )
    high = weight.astype(jnp.bfloat16)
    low = (weight - high.astype(jnp.float32)).astype(jnp.bfloat16)
    moe = jnp.dot(high, returned, preferred_element_type=jnp.float32) + jnp.dot(
        low, returned, preferred_element_type=jnp.float32
    )
    return (resid_f + moe).astype(jnp.bfloat16)


def solution(mesh):
    placed = (
        P(("req", "exp"), None),
        P(("req", "exp"), None),
        P(("req", "exp"), None),
        P("req", None),
        P("req", None, None),
        P("req", None, None),
        P(),
        P(),
        P(("req", "exp"), None),
        P(("req", "exp"), None, None),
        P(("req", "exp"), None, None),
        P(("req", "exp"), None, None),
    )
    return jax.shard_map(
        on_device, mesh=mesh, in_specs=placed, out_specs=P(("req", "exp"), None), check_vma=False
    )
```

profile of v0, /device:TPU:34, one launch (start us, length us, event | category | flops | bytes accessed | tf_op | source)
XLA Modules:
  0.0 531.8 jit_solution(14392213772407807917)
XLA Ops:
  11.2 12.1 %all_gather.9 = bf16[1024,56]{0,1:T(8,128)(2,1)S(1)} all-gather(bf16[128,56]{0,1:T(8,128)(2,1)S(1)} %convolution_convert_fusion.3), channel_id=1, replica_groups=mesh['req'=8,'exp'=16] {'req'}, dimensions={0}, use_global_device_ids=true | all-gather | bytes 129024 | tf_op jit(solution)/shard_map/all_gather | solution.py:78
  25.1 16.3 %all-gather.3.cloned.1.call-done = bf16[1024,1280]{0,1:T(8,128)(2,1)} async-done(((bf16[128,1280]{0,1:T(8,128)(2,1)}), bf16[1024,1280]{0,1:T(8,128)(2,1)}) %all-gather.3.cloned.1.call-update) | async-done | bytes 2621456 | tf_op jit(solution)/shard_map/all_gather | solution.py:77
  41.4 16.3 %fusion = (f32[1024,2,5]{0,2,1:T(8,128)S(1)}, f32[2,896,1024,5]{2,1,3,0:T(8,128)}) fusion(pred[1024,896]{0,1:T(8,128)(4,1)S(1)} %bitcast_compare_fusion, bf16[896,2,128,1]{0,2,3,1:T(8,128)(2,1)S(1)} %bitcast.144, bf16[1024,2,5,128]{0,3,2,1:T(8,128)(2,1)} %bitcast.138), kind=kOutput, calls=%fused_computation.2 | convolution fusion | flops 2376325120 | bytes 40738816 | tf_op jit(solution)/shard_map/tgrd,kgd->tgrk/dot_general | solution.py:18
  60.0 15.7 %fusion.4 = f32[1024,2,5]{0,2,1:T(8,128)S(1)} fusion(f32[2,896,1024,5]{2,1,3,0:T(8,128)} %get-tuple-element.20, f32[1024,896]{0,1:T(8,128)S(1)} %bitcast.133, f32[1024,2,5]{0,2,1:T(8,128)S(1)} %get-tuple-element.14, pred[1024,896]{0,1:T(8,128)(4,1)S(1)} %bitcast_compare_fusion), kind=kLoop, calls=%fused_computation.6 | loop fusion | flops 45864960 | bytes 41369600 | tf_op jit(solution)/shard_map/reduce_sum | solution.py:26
  76.3 4.0 all-to-all-start.2
  82.1 3.8 all-to-all-done.2
  85.8 3.3 all-to-all-start
  89.2 17.4 %bitcast_add_fusion = f32[1024,2,5,128]{3,0,2,1:T(8,128)S(1)} fusion(f32[1024,2,5]{0,2,1:T(8,128)S(1)} %get-tuple-element.13, bf16[896,2,128,1]{0,2,3,1:T(8,128)(2,1)S(1)} %bitcast.150, f32[2,896,1024,5]{2,1,3,0:T(8,128)} %get-tuple-element.20, f32[1024,896]{0,1:T(8,128)} %bitcast.134, f32[1024,2,5]{0,2,1:T(8,128)S(1)} %get-tuple-element.14, ...), kind=kOutput, calls=%fused_computation.21 | convolution fusion | flops 2395996160 | bytes 47071232 | tf_op jit(solution)/shard_map/tgrk,kgd->tgrd/dot_general | solution.py:27
  109.4 5.0 all-to-all-start.1
  115.1 15.4 %all-gather.5.cloned.1.call-done = bf16[2048,512]{0,1:T(8,128)(2,1)} async-done(((bf16[128,512]{0,1:T(8,128)(2,1)}), bf16[2048,512]{0,1:T(8,128)(2,1)}) %all-gather.5.cloned.1.call-update) | async-done | bytes 2097168 | tf_op jit(solution)/shard_map/all_gather | solution.py:127
  133.2 5.8 %fusion.9 = (f32[128,2,5]{0,2,1:T(8,128)S(1)}, f32[2,2048,128,5]{2,1,3,0:T(8,128)}) fusion(pred[128,2048]{0,1:T(8,128)(4,1)S(1)} %get-tuple-element.17, bf16[2048,2,128,1]{0,2,3,1:T(8,128)(2,1)S(1)} %bitcast.141, bf16[128,2,5,128]{0,3,2,1:T(8,128)(2,1)S(1)} %bitcast.140), kind=kOutput, calls=%fused_computation.14 | convolution fusion | flops 678951680 | bytes 12129280 | tf_op jit(solution)/shard_map/tgrd,kgd->tgrk/dot_general | solution.py:18
  139.2 6.4 %fusion.13 = f32[128,2,5]{0,2,1:T(8,128)S(1)} fusion(f32[2,2048,128,5]{2,1,3,0:T(8,128)} %get-tuple-element.22, f32[128,2048]{0,1:T(8,128)S(1)} %get-tuple-element.18, f32[128,2,5]{0,2,1:T(8,128)S(1)} %copy.161, pred[128,2048]{0,1:T(8,128)(4,1)S(1)} %get-tuple-element.17), kind=kLoop, calls=%fused_computation.18 | loop fusion | flops 13105920 | bytes 11806720 | tf_op jit(solution)/shard_map/reduce_sum | solution.py:26
  145.7 29.6 %all-to-all-done.1 = f32[8,128,2,5,128]{4,1,3,2,0:T(8,128)} async-done(((f32[8,128,2,5,128]{4,1,3,2,0:T(8,128)}), f32[8,128,2,5,128]{4,1,3,2,0:T(8,128)}, u32[]{:S(2)}, u32[]{:S(2)}) %all-to-all-start.1) | async-done | bytes 5242912 | tf_op jit(solution)/shard_map/all_to_all | solution.py:114
  175.3 4.3 multiply_reduce_fusion
  181.8 7.9 %fusion.42 = bf16[128,2,5,128]{0,3,2,1:T(8,128)(2,1)S(1)} fusion(bf16[2048,2,128,1]{0,2,3,1:T(8,128)(2,1)} %bitcast.147, f32[2,2048,128,5]{2,1,3,0:T(8,128)} %get-tuple-element.22, f32[128,2048]{0,1:T(8,128)} %copy-done.4, f32[128,2,5]{0,2,1:T(8,128)S(1)} %copy.161, pred[128,2048]{0,1:T(8,128)(4,1)S(1)} %get-tuple-element.17, ...), kind=kOutput, calls=%fused_computation.49 | convolution fusion | flops 684851200 | bytes 13843456 | tf_op jit(solution)/shard_map/tgrk,kgd->tgrd/dot_general | solution.py:27
  191.0 3.2 convolution_convert_fusion.1
  194.3 126.3 %all_to_all.25 = bf16[128,16,2560]{2,1,0:T(8,128)(2,1)S(1)} all-to-all(bf16[128,16,2560]{2,1,0:T(8,128)(2,1)S(1)} %bitcast.130), channel_id=1, replica_groups=mesh['req'=8,'exp'=16] {'req','exp'}, dimensions={0} | all-to-all | bytes 20971520 | tf_op jit(solution)/shard_map/all_to_all | solution.py:175
  320.5 3.8 copy-done.2
  324.4 10.2 %fusion.21 = f32[2048,768]{1,0:T(8,128)} fusion(bf16[2048,2560]{1,0:T(8,128)(2,1)S(1)} %bitcast.136, bf16[1,2560,768]{2,1,0:T(8,128)(2,1)S(1)} %copy-done.8), kind=kOutput, calls=%fused_computation.27 | convolution fusion | flops 8053063680 | bytes 20709376 | tf_op jit(solution)/shard_map/dot_general | solution.py:178
  334.5 28.9 %convolution_convert_fusion = bf16[2048,2560]{1,0:T(8,128)(2,1)} fusion(f32[2048,768]{1,0:T(8,128)} %fusion.21, bf16[2048,2560]{1,0:T(8,128)(2,1)} %bitcast.137, bf16[1,768,2560]{2,1,0:T(8,128)(2,1)} %param.23, bf16[1,2560,768]{2,1,0:T(8,128)(2,1)} %param.22), kind=kOutput, calls=%fused_computation.10 | convolution fusion | flops 16120807424 | bytes 35127296 | tf_op jit(solution)/shard_map/dot_general | solution.py:182
  363.5 6.7 %all-to-all-start.4 = ((bf16[128,16,2560]{2,1,0:T(8,128)(2,1)}), bf16[128,16,2560]{2,1,0:T(8,128)(2,1)}, u32[]{:S(2)}, u32[]{:S(2)}) async-start(bf16[128,16,2560]{2,1,0:T(8,128)(2,1)} %bitcast.135), calls=%async_computation.4 | async-start | bytes 20971520 | tf_op jit(solution)/shard_map/all_to_all | solution.py:181
  371.0 141.3 %all-to-all-done.4 = bf16[128,16,2560]{2,1,0:T(8,128)(2,1)} async-done(((bf16[128,16,2560]{2,1,0:T(8,128)(2,1)}), bf16[128,16,2560]{2,1,0:T(8,128)(2,1)}, u32[]{:S(2)}, u32[]{:S(2)}) %all-to-all-start.4) | async-done | bytes 10485792 | tf_op jit(solution)/shard_map/all_to_all | solution.py:181
  512.3 5.5 %fusion.70 = f32[128,2560]{1,0:T(8,128)S(1)} fusion(bf16[128,2048]{0,1:T(8,128)(2,1)S(1)} %bitcast.143, bf16[2048,2560]{1,0:T(8,128)(2,1)} %bitcast.34), kind=kOutput, calls=%fused_computation.101 | convolution fusion | flops 1342177280 | bytes 12320768 | tf_op jit(solution)/shard_map/dot_general | solution.py:198
  518.0 6.4 %fusion.24 = bf16[128,2560]{1,0:T(8,128)(2,1)} fusion(f32[128,2560]{1,0:T(8,128)S(1)} %fusion.70, bf16[128,2048]{0,1:T(8,128)(2,1)S(1)} %bitcast.142, bf16[2048,2560]{1,0:T(8,128)(2,1)} %bitcast.34, bf16[128,2560]{1,0:T(8,128)(2,1)S(1)} %fusion.25), kind=kOutput, calls=%fused_computation.32 | convolution fusion | flops 1343488000 | bytes 13631488 | tf_op jit(solution)/shard_map/dot_general | solution.py:198
  (81 shorter events, 21.0 us)
Async XLA Ops:
  7.4 362.8 %copy-start = (bf16[2560,64]{0,1:T(8,128)(2,1)S(1)}, bf16[2560,64]{0,1:T(8,128)(2,1)}, u32[]{:S(2)}) copy-start(bf16[2560,64]{0,1:T(8,128)(2,1)} %param.19) | copy-start | bytes 983044
  7.4 34.0 %all-gather.3.cloned.1.call-start = ((), (), s32[]{:S(2)}) async-start(), calls=%async_computation.5 | async-start | bytes 2949120 | tf_op jit(solution)/shard_map/all_gather | solution.py:77
  58.2 1.8 copy-start.1
  60.0 20.4 %copy-start.6 = (bf16[128,512]{1,0:T(8,128)(2,1)S(1)}, bf16[128,512]{1,0:T(8,128)(2,1)}, u32[]{:S(2)}) copy-start(bf16[128,512]{1,0:T(8,128)(2,1)} %param.14) | copy-start | bytes 393220
  76.3 9.5 %all-to-all-start.2 = ((f32[8,128,2,5]{1,2,3,0:T(2,128)}), f32[8,128,2,5]{1,2,3,0:T(2,128)S(1)}, u32[]{:S(2)}, u32[]{:S(2)}) async-start(f32[8,128,2,5]{1,2,3,0:T(2,128)} %copy.164), calls=%async_computation.2 | async-start | bytes 81920 | tf_op jit(solution)/shard_map/all_to_all | solution.py:107
  80.3 50.2 %all-gather.5.cloned.1.call-start = ((), (), s32[]{:S(2)}) async-start(), calls=%async_computation.6 | async-start | bytes 2228224 | tf_op jit(solution)/shard_map/all_gather | solution.py:127
  85.8 23.6 %all-to-all-start = ((f32[8,128,2,5]{1,2,3,0:T(2,128)}), f32[8,128,2,5]{1,2,3,0:T(2,128)S(1)}, u32[]{:S(2)}, u32[]{:S(2)}) async-start(f32[8,128,2,5]{1,2,3,0:T(2,128)} %copy.144), calls=%async_computation | async-start | bytes 81920 | tf_op jit(solution)/shard_map/all_to_all | solution.py:100
  106.6 7.7 %copy-start.9 = (s32[1,4]{1,0:T(1,128)S(1)}, s32[1,4]{1,0:T(1,128)}, u32[]{:S(2)}) copy-start(s32[1,4]{1,0:T(1,128)} %param.15) | copy-start | bytes 52
  106.6 7.8 %copy-start.7 = (s32[128,6]{0,1:T(8,128)S(1)}, s32[128,6]{0,1:T(8,128)}, u32[]{:S(2)}) copy-start(s32[128,6]{0,1:T(8,128)} %param.20) | copy-start | bytes 9220
  109.4 23.9 %copy-start.3 = (bf16[128,1280]{0,1:T(8,128)(2,1)S(1)}, bf16[128,1280]{0,1:T(8,128)(2,1)}, u32[]{:S(2)}) copy-start(bf16[128,1280]{0,1:T(8,128)(2,1)} %copy.140) | copy-start | bytes 983044
  109.4 65.9 %all-to-all-start.1 = ((f32[8,128,2,5,128]{4,1,3,2,0:T(8,128)}), f32[8,128,2,5,128]{4,1,3,2,0:T(8,128)}, u32[]{:S(2)}, u32[]{:S(2)}) async-start(f32[8,128,2,5,128]{4,1,3,2,0:T(8,128)} %copy.158), calls=%async_computation.1 | async-start | bytes 10485760 | tf_op jit(solution)/shard_map/all_to_all | solution.py:114
  115.1 24.1 %copy-start.4 = (f32[128,2048]{0,1:T(8,128)}, f32[128,2048]{0,1:T(8,128)S(1)}, u32[]{:S(2)}) copy-start(f32[128,2048]{0,1:T(8,128)S(1)} %get-tuple-element.18) | copy-start | bytes 3145732
  175.3 14.4 %slice-start = ((s8[6553600]{0:T(1024)(128)(4,1)}), s8[2359296]{0:T(1024)(128)(4,1)S(1)}, s32[]{:S(2)}) async-start(s8[6553600]{0:T(1024)(128)(4,1)} %bitcast.131), calls=%async_computation.7 | async-start | bytes 4718592
  181.8 7.9 %slice-start.1 = ((s8[6553600]{0:T(1024)(128)(4,1)}), s8[4194304]{0:T(1024)(128)(4,1)S(1)}, s32[]{:S(2)}) async-start(s8[6553600]{0:T(1024)(128)(4,1)} %bitcast.131), calls=%async_computation.8 | async-start | bytes 8388608
  181.8 7.9 %copy-start.5 = (bf16[128,2560]{1,0:T(8,128)(2,1)S(1)}, bf16[128,2560]{1,0:T(8,128)(2,1)}, u32[]{:S(2)}) copy-start(bf16[128,2560]{1,0:T(8,128)(2,1)} %param.12) | copy-start | bytes 1966084
  194.3 130.1 %copy-start.8 = (bf16[1,2560,768]{2,1,0:T(8,128)(2,1)S(1)}, bf16[1,2560,768]{2,1,0:T(8,128)(2,1)}, u32[]{:S(2)}) copy-start(bf16[1,2560,768]{2,1,0:T(8,128)(2,1)} %param.21) | copy-start | bytes 11796484
  320.5 3.8 copy-start.2
  363.5 148.8 %all-to-all-start.4 = ((bf16[128,16,2560]{2,1,0:T(8,128)(2,1)}), bf16[128,16,2560]{2,1,0:T(8,128)(2,1)}, u32[]{:S(2)}, u32[]{:S(2)}) async-start(bf16[128,16,2560]{2,1,0:T(8,128)(2,1)} %bitcast.135), calls=%async_computation.4 | async-start | bytes 20971520 | tf_op jit(solution)/shard_map/all_to_all | solution.py:181
Sparse Core Ops, SparseCore 0:
  9.9 31.4 all-gather.2
Sparse Core Ops, SparseCore 1:
  82.9 47.5 all-gather.4
where the time goes:
time: 533 us; the launch traced here: 532 us
  waiting for transfers between devices  206 us (39%)
  blocking collectives  138 us (26%)
  matrix products  104 us (20%)
  other arithmetic  29.7 us (6%)
  local copies, waits for them, and re-layouts  19.7 us (4%)
  starting transfers between devices  19 us (4%)
  between operations  15.2 us (3%)
    all_to_all x1, waiting for transfers between devices, on_device(): lax.all_to_all(jnp.dot(inner, w_down[0], preferred_element_type=jnp.float...  141 us
    all_to_all x1, blocking collectives, on_device(): lax.all_to_all(outgoing, ('req', 'exp'), split_axis=0, concat_axis=0, til...  126 us
    all_to_all x1, waiting for transfers between devices, on_device(): lax.all_to_all(summed_output.reshape(request_count, token_index, KEY_VALU...  29.6 us
    dot_general x1, matrix products, on_device(): jnp.dot(inner, w_down[0], preferred_element_type=jnp.float32)  28.9 us
    dot_general x2, matrix products, fold_scores(): jnp.einsum('tgrk,kgd->tgrd', expo.astype(jnp.bfloat16), value_rows, prefe...  25.3 us
    dot_general x2, matrix products, fold_scores(): jnp.einsum('tgrd,kgd->tgrk', query_matrix, key_rows, preferred_element_ty...  22.1 us
    reduce_sum x2, other arithmetic, fold_scores(): grand_total = decay * grand_total + jnp.sum(expo, axis=-1)  22.1 us
    all_gather x1, waiting for transfers between devices, on_device(): lax.all_gather(queries, 'req', axis=0, tiled=True)  16.3 us
  transfers between devices with their start and end apart: 6, of which 5 were waited for; matrix products, arithmetic and copies ran while one was open for 8% of the time, Pallas kernels for 0%

commit v1 on v0

--- a/solution.py
+++ b/solution.py
@@ -124,7 +124,12 @@
     highest = jnp.max(peaks, axis=0)
     factor = jnp.exp(peaks - highest[None])
     carry = (highest, jnp.sum(factor * totals, axis=0), jnp.sum(factor[..., None] * sums, axis=0))
-    segment = lax.all_gather(suffix_kv, "exp", axis=0, tiled=True)
+    ring = [suffix_kv]
+    for hop in range(15):
+        ring.append(lax.ppermute(ring[-1], "exp", [(dev, (dev + 1) % 16) for dev in range(16)]))
+    segment = jnp.roll(
+        jnp.concatenate(ring[::-1], axis=0), (lax.axis_index("exp") + 1) * ring[0].shape[0], axis=0
+    )
     token_count = segment.shape[0]
     keypos = jnp.arange(token_count, dtype=jnp.int32)
     weights = (

time: 533 us -> 661 us (1.24); the launches traced: 532 us -> 652 us
  waiting for transfers between devices: 206 us -> 247 us
  local copies, waits for them, and re-layouts: 19.7 us -> 57.3 us
  starting transfers between devices: 19 us -> 43.3 us
  blocking collectives: 138 us -> 156 us
    ppermute x0 -> x15, waiting for transfers between devices: none -> 77 us  [on_device(): lax.ppermute(ring[-1], 'exp', [(dev, (dev + 1) % 16) for dev in range(16)])]
    unnamed x26 -> x111, local copies, waits for them, and re-layouts: 8.36 us -> 42.1 us
    all_to_all x1, blocking collectives: 126 us -> 144 us  [on_device(): lax.all_to_all(outgoing, ('req', 'exp'), split_axis=0, concat_axis=0, til...]
    all_gather x1, waiting for transfers between devices: 16.3 us -> 0.01 us  [on_device(): lax.all_gather(queries, 'req', axis=0, tiled=True)]
    all_gather x1 -> x0, waiting for transfers between devices: 15.4 us -> none  [on_device(): segment = lax.all_gather(suffix_kv, 'exp', axis=0, tiled=True)]
    all_to_all x1, starting transfers between devices: 3.34 us -> 15.2 us  [on_device(): lax.all_to_all(running_maximum.reshape(request_count, token_index, KEY_VA...]
    ppermute x0 -> x15, starting transfers between devices: none -> 11.7 us  [on_device(): lax.ppermute(ring[-1], 'exp', [(dev, (dev + 1) % 16) for dev in range(16)])]
  transfers between devices with their start and end apart: 6 -> 20, of which waited for: 5 -> 16; matrix products, arithmetic and copies ran while one was open for 8% -> 15% of each run, Pallas kernels for 0% -> 0%
where the time goes in v1:
time: 661 us; the launch traced here: 652 us
  waiting for transfers between devices  247 us (37%)
  blocking collectives  156 us (24%)
  matrix products  104 us (16%)
  local copies, waits for them, and re-layouts  57.3 us (9%)
  starting transfers between devices  43.3 us (7%)
  other arithmetic  30.2 us (5%)
  between operations  14.3 us (2%)
    all_to_all x1, blocking collectives, on_device(): lax.all_to_all(outgoing, ('req', 'exp'), split_axis=0, concat_axis=0, til...  144 us
    all_to_all x1, waiting for transfers between devices, on_device(): lax.all_to_all(jnp.dot(inner, w_down[0], preferred_element_type=jnp.float...  141 us
    ppermute x15, waiting for transfers between devices, on_device(): lax.ppermute(ring[-1], 'exp', [(dev, (dev + 1) % 16) for dev in range(16)])  77 us
    unnamed x111, local copies, waits for them, and re-layouts  42.1 us
    dot_general x1, matrix products, on_device(): jnp.dot(inner, w_down[0], preferred_element_type=jnp.float32)  29 us
    all_to_all x1, waiting for transfers between devices, on_device(): lax.all_to_all(summed_output.reshape(request_count, token_index, KEY_VALU...  28.6 us
    dot_general x2, matrix products, fold_scores(): jnp.einsum('tgrk,kgd->tgrd', expo.astype(jnp.bfloat16), value_rows, prefe...  25.4 us
    dot_general x2, matrix products, fold_scores(): jnp.einsum('tgrd,kgd->tgrk', query_matrix, key_rows, preferred_element_ty...  22.3 us
  transfers between devices with their start and end apart: 20, of which 16 were waited for; matrix products, arithmetic and copies ran while one was open for 15% of the time, Pallas kernels for 0%

profile of v1, /device:TPU:34, one launch (start us, length us, event | category | flops | bytes accessed | tf_op | source)
XLA Modules:
  0.0 652.0 jit_solution(9487197978273803084)
XLA Ops:
  19.4 6.2 collective-permute-done.2
  25.6 7.1 %collective-permute-done.3 = bf16[128,512]{0,1:T(8,128)(2,1)S(1)} collective-permute-done((bf16[128,512]{0,1:T(8,128)(2,1)S(1)}, bf16[128,512]{0,1:T(8,128)(2,1)S(1)}, u32[]{:S(2)}, u32[]{:S(2)}) %collective-permute-start.3) | collective-permute-done | bytes 131104 | tf_op jit(solution)/shard_map/ppermute | solution.py:129
  32.7 7.8 %collective-permute-done.4 = bf16[128,512]{0,1:T(8,128)(2,1)S(1)} collective-permute-done((bf16[128,512]{0,1:T(8,128)(2,1)S(1)}, bf16[128,512]{0,1:T(8,128)(2,1)S(1)}, u32[]{:S(2)}, u32[]{:S(2)}) %collective-permute-start.4) | collective-permute-done | bytes 131104 | tf_op jit(solution)/shard_map/ppermute | solution.py:129
  41.3 7.5 %collective-permute-done.5 = bf16[128,512]{0,1:T(8,128)(2,1)S(1)} collective-permute-done((bf16[128,512]{0,1:T(8,128)(2,1)S(1)}, bf16[128,512]{0,1:T(8,128)(2,1)S(1)}, u32[]{:S(2)}, u32[]{:S(2)}) %collective-permute-start.5) | collective-permute-done | bytes 131104 | tf_op jit(solution)/shard_map/ppermute | solution.py:129
  49.4 6.2 collective-permute-done.6
  55.9 6.8 %collective-permute-done.7 = bf16[128,512]{0,1:T(8,128)(2,1)S(1)} collective-permute-done((bf16[128,512]{0,1:T(8,128)(2,1)S(1)}, bf16[128,512]{0,1:T(8,128)(2,1)S(1)}, u32[]{:S(2)}, u32[]{:S(2)}) %collective-permute-start.7) | collective-permute-done | bytes 131104 | tf_op jit(solution)/shard_map/ppermute | solution.py:129
  63.0 6.7 %collective-permute-done.8 = bf16[128,512]{0,1:T(8,128)(2,1)S(1)} collective-permute-done((bf16[128,512]{0,1:T(8,128)(2,1)S(1)}, bf16[128,512]{0,1:T(8,128)(2,1)S(1)}, u32[]{:S(2)}, u32[]{:S(2)}) %collective-permute-start.8) | collective-permute-done | bytes 131104 | tf_op jit(solution)/shard_map/ppermute | solution.py:129
  77.0 12.1 %all_gather.6 = bf16[1024,56]{0,1:T(8,128)(2,1)S(1)} all-gather(bf16[128,56]{0,1:T(8,128)(2,1)S(1)} %convolution_convert_fusion.3), channel_id=1, replica_groups=mesh['req'=8,'exp'=16] {'req'}, dimensions={0}, use_global_device_ids=true | all-gather | bytes 129024 | tf_op jit(solution)/shard_map/all_gather | solution.py:78
  112.4 7.2 %collective-permute-done.14 = bf16[128,512]{0,1:T(8,128)(2,1)S(1)} collective-permute-done((bf16[128,512]{0,1:T(8,128)(2,1)S(1)}, bf16[128,512]{0,1:T(8,128)(2,1)S(1)}, u32[]{:S(2)}, u32[]{:S(2)}) %collective-permute-start.14) | collective-permute-done | bytes 131104 | tf_op jit(solution)/shard_map/ppermute | solution.py:129
  135.8 16.5 %fusion = (f32[1024,2,5]{0,2,1:T(8,128)S(1)}, f32[2,896,1024,5]{2,1,3,0:T(8,128)}) fusion(pred[1024,896]{0,1:T(8,128)(4,1)S(1)} %bitcast_compare_fusion, bf16[896,2,128,1]{0,2,3,1:T(8,128)(2,1)} %bitcast.144, bf16[1024,2,5,128]{0,3,2,1:T(8,128)(2,1)} %bitcast.138), kind=kOutput, calls=%fused_computation.2 | convolution fusion | flops 2376325120 | bytes 40738816 | tf_op jit(solution)/shard_map/tgrd,kgd->tgrk/dot_general | solution.py:18
  153.0 15.2 %all-to-all-start = ((f32[8,128,2,5]{1,2,3,0:T(2,128)}), f32[8,128,2,5]{1,2,3,0:T(2,128)S(1)}, u32[]{:S(2)}, u32[]{:S(2)}) async-start(f32[8,128,2,5]{1,2,3,0:T(2,128)} %copy.154), calls=%async_computation | async-start | bytes 81920 | tf_op jit(solution)/shard_map/all_to_all | solution.py:100
  170.5 15.6 %fusion.4 = f32[1024,2,5]{0,2,1:T(8,128)S(1)} fusion(f32[2,896,1024,5]{2,1,3,0:T(8,128)} %get-tuple-element.20, f32[1024,896]{0,1:T(8,128)S(1)} %bitcast.133, f32[1024,2,5]{0,2,1:T(8,128)S(1)} %get-tuple-element.14, pred[1024,896]{0,1:T(8,128)(4,1)S(1)} %bitcast_compare_fusion), kind=kLoop, calls=%fused_computation.6 | loop fusion | flops 45864960 | bytes 41369600 | tf_op jit(solution)/shard_map/reduce_sum | solution.py:26
  191.4 17.5 %bitcast_add_fusion = f32[1024,2,5,128]{3,0,2,1:T(8,128)S(1)} fusion(f32[1024,2,5]{0,2,1:T(8,128)S(1)} %get-tuple-element.13, bf16[896,2,128,1]{0,2,3,1:T(8,128)(2,1)} %bitcast.150, f32[2,896,1024,5]{2,1,3,0:T(8,128)} %get-tuple-element.20, f32[1024,896]{0,1:T(8,128)} %bitcast.134, f32[1024,2,5]{0,2,1:T(8,128)S(1)} %get-tuple-element.14, ...), kind=kOutput, calls=%fused_computation.21 | convolution fusion | flops 2395996160 | bytes 47071232 | tf_op jit(solution)/shard_map/tgrk,kgd->tgrd/dot_general | solution.py:27
  236.6 5.9 fusion.9
  242.6 6.4 fusion.13
  249.0 28.6 %all-to-all-done.1 = f32[8,128,2,5,128]{4,1,3,2,0:T(8,128)} async-done(((f32[8,128,2,5,128]{4,1,3,2,0:T(8,128)}), f32[8,128,2,5,128]{4,1,3,2,0:T(8,128)}, u32[]{:S(2)}, u32[]{:S(2)}) %all-to-all-start.1) | async-done | bytes 5242912 | tf_op jit(solution)/shard_map/all_to_all | solution.py:114
  284.1 7.9 %fusion.42 = bf16[128,2,5,128]{0,3,2,1:T(8,128)(2,1)S(1)} fusion(bf16[2048,2,128,1]{0,2,3,1:T(8,128)(2,1)} %bitcast.147, f32[2,2048,128,5]{2,1,3,0:T(8,128)} %get-tuple-element.22, f32[128,2048]{0,1:T(8,128)} %copy-done.4, f32[128,2,5]{0,2,1:T(8,128)S(1)} %copy.173, pred[128,2048]{0,1:T(8,128)(4,1)S(1)} %get-tuple-element.17, ...), kind=kOutput, calls=%fused_computation.49 | convolution fusion | flops 684851200 | bytes 13843456 | tf_op jit(solution)/shard_map/tgrk,kgd->tgrd/dot_general | solution.py:27
  296.6 144.1 %all_to_all.25 = bf16[128,16,2560]{2,1,0:T(8,128)(2,1)S(1)} all-to-all(bf16[128,16,2560]{2,1,0:T(8,128)(2,1)S(1)} %bitcast.130), channel_id=1, replica_groups=mesh['req'=8,'exp'=16] {'req','exp'}, dimensions={0} | all-to-all | bytes 20971520 | tf_op jit(solution)/shard_map/all_to_all | solution.py:180
  444.6 10.2 %fusion.21 = f32[2048,768]{1,0:T(8,128)} fusion(bf16[2048,2560]{1,0:T(8,128)(2,1)S(1)} %bitcast.136, bf16[1,2560,768]{2,1,0:T(8,128)(2,1)S(1)} %copy-done.36), kind=kOutput, calls=%fused_computation.27 | convolution fusion | flops 8053063680 | bytes 20709376 | tf_op jit(solution)/shard_map/dot_general | solution.py:183
  454.8 29.0 %convolution_convert_fusion = bf16[2048,2560]{1,0:T(8,128)(2,1)} fusion(f32[2048,768]{1,0:T(8,128)} %fusion.21, bf16[2048,2560]{1,0:T(8,128)(2,1)} %bitcast.137, bf16[1,768,2560]{2,1,0:T(8,128)(2,1)} %param.23, bf16[1,2560,768]{2,1,0:T(8,128)(2,1)} %param.22), kind=kOutput, calls=%fused_computation.10 | convolution fusion | flops 16120807424 | bytes 35127296 | tf_op jit(solution)/shard_map/dot_general | solution.py:187
  483.7 6.8 %all-to-all-start.4 = ((bf16[128,16,2560]{2,1,0:T(8,128)(2,1)}), bf16[128,16,2560]{2,1,0:T(8,128)(2,1)}, u32[]{:S(2)}, u32[]{:S(2)}) async-start(bf16[128,16,2560]{2,1,0:T(8,128)(2,1)} %bitcast.135), calls=%async_computation.4 | async-start | bytes 20971520 | tf_op jit(solution)/shard_map/all_to_all | solution.py:186
  491.4 141.3 %all-to-all-done.4 = bf16[128,16,2560]{2,1,0:T(8,128)(2,1)} async-done(((bf16[128,16,2560]{2,1,0:T(8,128)(2,1)}), bf16[128,16,2560]{2,1,0:T(8,128)(2,1)}, u32[]{:S(2)}, u32[]{:S(2)}) %all-to-all-start.4) | async-done | bytes 10485792 | tf_op jit(solution)/shard_map/all_to_all | solution.py:186
  632.8 5.5 fusion.69
  638.4 6.4 fusion.24
  (194 shorter events, 113.3 us)
Async XLA Ops:
  6.5 484.0 %copy-start = (bf16[2560,64]{0,1:T(8,128)(2,1)S(1)}, bf16[2560,64]{0,1:T(8,128)(2,1)}, u32[]{:S(2)}) copy-start(bf16[2560,64]{0,1:T(8,128)(2,1)} %param.19) | copy-start | bytes 983044
  6.5 89.5 %copy-start.33 = (s32[128,6]{0,1:T(8,128)S(1)}, s32[128,6]{0,1:T(8,128)}, u32[]{:S(2)}) copy-start(s32[128,6]{0,1:T(8,128)} %param.20) | copy-start | bytes 9220
  6.5 129.3 %all-gather.2.cloned.1.call-start = ((), (), s32[]{:S(2)}) async-start(), calls=%async_computation.5 | async-start | bytes 2949120 | tf_op jit(solution)/shard_map/all_gather | solution.py:77
  7.6 5.3 collective-permute-start
  12.9 5.6 collective-permute-start.1
  18.5 7.1 %collective-permute-start.2 = (bf16[128,512]{0,1:T(8,128)(2,1)S(1)}, bf16[128,512]{0,1:T(8,128)(2,1)S(1)}, u32[]{:S(2)}, u32[]{:S(2)}) collective-permute-start(bf16[128,512]{0,1:T(8,128)(2,1)S(1)} %collective-permute-done.1), channel_id=1, source_target_pairs={{0,1},{1,2},{2,3},{3,4},{4,5},{5,6},{6,7},{7,8},{8,9},{9,10},{10,1... | collective-permute-start | bytes 393224 | tf_op jit(solution)/shard_map/ppermute | solution.py:129
  25.6 7.1 %collective-permute-start.3 = (bf16[128,512]{0,1:T(8,128)(2,1)S(1)}, bf16[128,512]{0,1:T(8,128)(2,1)S(1)}, u32[]{:S(2)}, u32[]{:S(2)}) collective-permute-start(bf16[128,512]{0,1:T(8,128)(2,1)S(1)} %collective-permute-done.2), channel_id=1, source_target_pairs={{0,1},{1,2},{2,3},{3,4},{4,5},{5,6},{6,7},{7,8},{8,9},{9,10},{10,1... | collective-permute-start | bytes 393224 | tf_op jit(solution)/shard_map/ppermute | solution.py:129
  32.7 7.8 %collective-permute-start.4 = (bf16[128,512]{0,1:T(8,128)(2,1)S(1)}, bf16[128,512]{0,1:T(8,128)(2,1)S(1)}, u32[]{:S(2)}, u32[]{:S(2)}) collective-permute-start(bf16[128,512]{0,1:T(8,128)(2,1)S(1)} %collective-permute-done.3), channel_id=1, source_target_pairs={{0,1},{1,2},{2,3},{3,4},{4,5},{5,6},{6,7},{7,8},{8,9},{9,10},{10,1... | collective-permute-start | bytes 393224 | tf_op jit(solution)/shard_map/ppermute | solution.py:129
  40.4 8.3 %collective-permute-start.5 = (bf16[128,512]{0,1:T(8,128)(2,1)S(1)}, bf16[128,512]{0,1:T(8,128)(2,1)S(1)}, u32[]{:S(2)}, u32[]{:S(2)}) collective-permute-start(bf16[128,512]{0,1:T(8,128)(2,1)S(1)} %collective-permute-done.4), channel_id=1, source_target_pairs={{0,1},{1,2},{2,3},{3,4},{4,5},{5,6},{6,7},{7,8},{8,9},{9,10},{10,1... | collective-permute-start | bytes 393224 | tf_op jit(solution)/shard_map/ppermute | solution.py:129
  48.8 6.9 %collective-permute-start.6 = (bf16[128,512]{0,1:T(8,128)(2,1)S(1)}, bf16[128,512]{0,1:T(8,128)(2,1)S(1)}, u32[]{:S(2)}, u32[]{:S(2)}) collective-permute-start(bf16[128,512]{0,1:T(8,128)(2,1)S(1)} %collective-permute-done.5), channel_id=1, source_target_pairs={{0,1},{1,2},{2,3},{3,4},{4,5},{5,6},{6,7},{7,8},{8,9},{9,10},{10,1... | collective-permute-start | bytes 393224 | tf_op jit(solution)/shard_map/ppermute | solution.py:129
  55.7 7.0 %collective-permute-start.7 = (bf16[128,512]{0,1:T(8,128)(2,1)S(1)}, bf16[128,512]{0,1:T(8,128)(2,1)S(1)}, u32[]{:S(2)}, u32[]{:S(2)}) collective-permute-start(bf16[128,512]{0,1:T(8,128)(2,1)S(1)} %collective-permute-done.6), channel_id=1, source_target_pairs={{0,1},{1,2},{2,3},{3,4},{4,5},{5,6},{6,7},{7,8},{8,9},{9,10},{10,1... | collective-permute-start | bytes 393224 | tf_op jit(solution)/shard_map/ppermute | solution.py:129
  62.7 7.1 %collective-permute-start.8 = (bf16[128,512]{0,1:T(8,128)(2,1)S(1)}, bf16[128,512]{0,1:T(8,128)(2,1)S(1)}, u32[]{:S(2)}, u32[]{:S(2)}) collective-permute-start(bf16[128,512]{0,1:T(8,128)(2,1)S(1)} %collective-permute-done.7), channel_id=1, source_target_pairs={{0,1},{1,2},{2,3},{3,4},{4,5},{5,6},{6,7},{7,8},{8,9},{9,10},{10,1... | collective-permute-start | bytes 393224 | tf_op jit(solution)/shard_map/ppermute | solution.py:129
  63.0 179.6 %copy-start.4 = (f32[128,2048]{0,1:T(8,128)}, f32[128,2048]{0,1:T(8,128)S(1)}, u32[]{:S(2)}) copy-start(f32[128,2048]{0,1:T(8,128)S(1)} %get-tuple-element.18) | copy-start | bytes 3145732
  69.7 7.1 %collective-permute-start.9 = (bf16[128,512]{0,1:T(8,128)(2,1)S(1)}, bf16[128,512]{0,1:T(8,128)(2,1)S(1)}, u32[]{:S(2)}, u32[]{:S(2)}) collective-permute-start(bf16[128,512]{0,1:T(8,128)(2,1)S(1)} %collective-permute-done.8), channel_id=1, source_target_pairs={{0,1},{1,2},{2,3},{3,4},{4,5},{5,6},{6,7},{7,8},{8,9},{9,10},{10,1... | collective-permute-start | bytes 393224 | tf_op jit(solution)/shard_map/ppermute | solution.py:129
  76.8 12.3 %collective-permute-start.10 = (bf16[128,512]{0,1:T(8,128)(2,1)S(1)}, bf16[128,512]{0,1:T(8,128)(2,1)}, u32[]{:S(2)}, u32[]{:S(2)}) collective-permute-start(bf16[128,512]{0,1:T(8,128)(2,1)S(1)} %collective-permute-done.9), channel_id=1, source_target_pairs={{0,1},{1,2},{2,3},{3,4},{4,5},{5,6},{6,7},{7,8},{8,9},{9,10},{10,1... | collective-permute-start | bytes 393224 | tf_op jit(solution)/shard_map/ppermute | solution.py:129
  89.2 8.5 %collective-permute-start.11 = (bf16[128,512]{0,1:T(8,128)(2,1)}, bf16[128,512]{0,1:T(8,128)(2,1)}, u32[]{:S(2)}, u32[]{:S(2)}) collective-permute-start(bf16[128,512]{0,1:T(8,128)(2,1)} %collective-permute-done.10), channel_id=1, source_target_pairs={{0,1},{1,2},{2,3},{3,4},{4,5},{5,6},{6,7},{7,8},{8,9},{9,10},{10,1... | collective-permute-start | bytes 393224 | tf_op jit(solution)/shard_map/ppermute | solution.py:129
  97.6 7.8 %collective-permute-start.12 = (bf16[128,512]{0,1:T(8,128)(2,1)}, bf16[128,512]{0,1:T(8,128)(2,1)S(1)}, u32[]{:S(2)}, u32[]{:S(2)}) collective-permute-start(bf16[128,512]{0,1:T(8,128)(2,1)} %collective-permute-done.11), channel_id=1, source_target_pairs={{0,1},{1,2},{2,3},{3,4},{4,5},{5,6},{6,7},{7,8},{8,9},{9,10},{10,1... | collective-permute-start | bytes 393224 | tf_op jit(solution)/shard_map/ppermute | solution.py:129
  105.4 6.8 %collective-permute-start.13 = (bf16[128,512]{0,1:T(8,128)(2,1)S(1)}, bf16[128,512]{0,1:T(8,128)(2,1)S(1)}, u32[]{:S(2)}, u32[]{:S(2)}) collective-permute-start(bf16[128,512]{0,1:T(8,128)(2,1)S(1)} %collective-permute-done.12), channel_id=1, source_target_pairs={{0,1},{1,2},{2,3},{3,4},{4,5},{5,6},{6,7},{7,8},{8,9},{9,10},{10,1... | collective-permute-start | bytes 393224 | tf_op jit(solution)/shard_map/ppermute | solution.py:129
  112.2 7.3 %collective-permute-start.14 = (bf16[128,512]{0,1:T(8,128)(2,1)S(1)}, bf16[128,512]{0,1:T(8,128)(2,1)S(1)}, u32[]{:S(2)}, u32[]{:S(2)}) collective-permute-start(bf16[128,512]{0,1:T(8,128)(2,1)S(1)} %collective-permute-done.13), channel_id=1, source_target_pairs={{0,1},{1,2},{2,3},{3,4},{4,5},{5,6},{6,7},{7,8},{8,9},{9,10},{10,1... | collective-permute-start | bytes 393224 | tf_op jit(solution)/shard_map/ppermute | solution.py:129
  153.0 33.8 %all-to-all-start = ((f32[8,128,2,5]{1,2,3,0:T(2,128)}), f32[8,128,2,5]{1,2,3,0:T(2,128)S(1)}, u32[]{:S(2)}, u32[]{:S(2)}) async-start(f32[8,128,2,5]{1,2,3,0:T(2,128)} %copy.154), calls=%async_computation | async-start | bytes 81920 | tf_op jit(solution)/shard_map/all_to_all | solution.py:100
  186.8 24.9 %all-to-all-start.2 = ((f32[8,128,2,5]{1,2,3,0:T(2,128)}), f32[8,128,2,5]{1,2,3,0:T(2,128)S(1)}, u32[]{:S(2)}, u32[]{:S(2)}) async-start(f32[8,128,2,5]{1,2,3,0:T(2,128)} %copy.176), calls=%async_computation.2 | async-start | bytes 81920 | tf_op jit(solution)/shard_map/all_to_all | solution.py:107
  211.7 66.0 %all-to-all-start.1 = ((f32[8,128,2,5,128]{4,1,3,2,0:T(8,128)}), f32[8,128,2,5,128]{4,1,3,2,0:T(8,128)}, u32[]{:S(2)}, u32[]{:S(2)}) async-start(f32[8,128,2,5,128]{4,1,3,2,0:T(8,128)} %copy.170), calls=%async_computation.1 | async-start | bytes 10485760 | tf_op jit(solution)/shard_map/all_to_all | solution.py:114
  296.6 147.9 %copy-start.36 = (bf16[1,2560,768]{2,1,0:T(8,128)(2,1)S(1)}, bf16[1,2560,768]{2,1,0:T(8,128)(2,1)}, u32[]{:S(2)}) copy-start(bf16[1,2560,768]{2,1,0:T(8,128)(2,1)} %param.21) | copy-start | bytes 11796484
  483.7 148.9 %all-to-all-start.4 = ((bf16[128,16,2560]{2,1,0:T(8,128)(2,1)}), bf16[128,16,2560]{2,1,0:T(8,128)(2,1)}, u32[]{:S(2)}, u32[]{:S(2)}) async-start(bf16[128,16,2560]{2,1,0:T(8,128)(2,1)} %bitcast.135), calls=%async_computation.4 | async-start | bytes 20971520 | tf_op jit(solution)/shard_map/all_to_all | solution.py:186
  (35 other events, 889.3 us)
Sparse Core Ops, SparseCore 0:
  16.4 33.2 all-gather.1
